TPU v7x, 256 devices: a whole 4x4x8 slice. The times are simulated.
256 devices in a mesh: kv: 8 (over x, core), seq: 32 (over z, y).
Axes of the slice: x: 4, y: 4, z: 8, core: 2. Of those that a mesh axis runs over, the one named last changes fastest.
Arguments:
- hidden_states: bfloat16 [6144, 2048], P('seq')
- attn_gain: float32 [2048], replicated, may hold values from 0.5 to 1.5
- w_q: bfloat16 [2048, 2048], P(None, 'kv')
- w_k: bfloat16 [2048, 512], P(None, 'kv')
- w_v: bfloat16 [2048, 512], P(None, 'kv'), may hold values from -0.125 to 0.125
- w_o: bfloat16 [2048, 2048], P('kv'), may hold values from -0.125 to 0.125
- final_gain: float32 [2048], replicated, may hold values from 0.5 to 1.5
- w_head: bfloat16 [2048, 49408], P(None, ('kv', 'seq'))
- doc_lengths: int32 [26], replicated, may hold values from 1 to 3072, as said below
- target_ids: int32 [6144], replicated, may hold values from 0 to 49154, as said below
- vocab_mask: int32 [49408], P(('kv', 'seq')), may hold values from 0 to 1, as said below
Outputs:
- log_probs: float32 [6144], P('seq')
- entropies: float32 [6144], P('seq')
Inputs may be any that keep to these rules, and one draw needn't show every extreme that they name: `doc_lengths`: they sum to 6144; one is 3072, one more is over 1536, every other is under 64. `target_ids`: each names an entry whose vocab_mask is 1. `vocab_mask`: entries from 49155 on are 0.
All inputs are finite; a program needn't handle non-finite values.
Results may differ from a plain program's by a relative error of at most 0.0045.
Values may be sent and summed in bfloat16 or wider, within the bound.
No kernel may reach another device: no remote copies, remote signals or barrier semaphores. Data moves between devices by JAX's collectives and lax.ppermute only.
A program may use at most 128 MiB of HBM per device.

v0:
```python
import math
import jax
import jax.numpy as jnp
from jax import lax
from jax.sharding import Mesh, PartitionSpec as P

HEAD_DIM = 64
ROPE_THETA = 10000000.0
NORM_EPS = 1e-05
NEG_FILL = -1e30
ATTN_SCALE = 0.015625
RESID_SCALE = 5.0
LOGIT_SCALE = 0.125


def rms_norm(values, gain_vec):
    return (
        values * lax.rsqrt(jnp.mean(values * values, axis=-1, keepdims=True) + NORM_EPS) * gain_vec
    )


def rotate(values, positions):
    half_dim = values.shape[-1] // 2
    inverse = jnp.exp(
        jnp.arange(half_dim, dtype=jnp.float32) * (-2.0 * math.log(ROPE_THETA) / values.shape[-1])
    )
    angles = positions.astype(jnp.float32)[:, None] * inverse[None, :]
    cos_val = jnp.cos(angles)[:, None, :]
    sine_val = jnp.sin(angles)[:, None, :]
    lower_half = values[..., :half_dim]
    upper_half = values[..., half_dim:]
    return jnp.concatenate(
        [
            lower_half * cos_val - upper_half * sine_val,
            upper_half * cos_val + lower_half * sine_val,
        ],
        axis=-1,
    )


def local(
    hidden_states,
    attn_gain,
    w_q,
    w_k,
    w_v,
    w_o,
    final_gain,
    w_head,
    doc_lengths,
    target_ids,
    vocab_mask,
):
    tok_rows = hidden_states.shape[0]
    seq_index = lax.axis_index(("z", "y"))
    kv_local = w_k.shape[1] // HEAD_DIM
    q_local = w_q.shape[1] // HEAD_DIM
    group_size = q_local // kv_local
    key_width = kv_local * HEAD_DIM
    stream = hidden_states.astype(jnp.float32)
    normed_in = rms_norm(stream, attn_gain).astype(jnp.bfloat16)
    queries = jnp.dot(normed_in, w_q, preferred_element_type=jnp.float32)
    key_proj = jnp.dot(normed_in, w_k, preferred_element_type=jnp.float32)
    value_proj = jnp.dot(normed_in, w_v, preferred_element_type=jnp.float32)
    token_pos = seq_index * tok_rows + jnp.arange(tok_rows, dtype=jnp.int32)
    doc_ends = jnp.cumsum(doc_lengths)
    doc_starts = doc_ends - doc_lengths
    doc_start = jnp.max(
        jnp.where(doc_starts[None, :] <= token_pos[:, None], doc_starts[None, :], 0), axis=1
    )
    positions = token_pos - doc_start
    rotated_q = rotate(queries.reshape(tok_rows, q_local, HEAD_DIM), positions).astype(jnp.bfloat16)
    rotated_q = rotated_q.reshape(tok_rows, kv_local, group_size, HEAD_DIM)
    rotated_k = rotate(key_proj.reshape(tok_rows, kv_local, HEAD_DIM), positions).astype(
        jnp.bfloat16
    )
    packed = jnp.concatenate(
        [rotated_k.reshape(tok_rows, key_width), value_proj.astype(jnp.bfloat16)], axis=1
    )
    earliest = doc_start[0]
    latest = token_pos[tok_rows - 1]
    initial = (
        jnp.full((kv_local, group_size, tok_rows), NEG_FILL, jnp.float32),
        jnp.zeros((kv_local, group_size, tok_rows), jnp.float32),
        jnp.zeros((kv_local, group_size, tok_rows, HEAD_DIM), jnp.float32),
    )
    shard_rows = lax.all_gather(packed, ("z", "y"), axis=0, tiled=True)
    offset = jnp.int32(0)
    row_count = shard_rows.shape[0]
    key_pos = jnp.arange(row_count, dtype=jnp.int32)

    def update(current):
        top_score, totals, context_sum = current
        key_rows = shard_rows[:, :key_width].reshape(row_count, kv_local, HEAD_DIM)
        value_rows = shard_rows[:, key_width:].reshape(row_count, kv_local, HEAD_DIM)
        scores = (
            jnp.einsum("tkgd,skd->kgts", rotated_q, key_rows, preferred_element_type=jnp.float32)
            * ATTN_SCALE
        )
        allowed = (key_pos[None, :] >= doc_start[:, None]) & (
            key_pos[None, :] <= token_pos[:, None]
        )
        scores = jnp.where(allowed, scores, NEG_FILL)
        new_top = jnp.maximum(top_score, jnp.max(scores, axis=-1))
        weights = jnp.where(allowed, jnp.exp(scores - new_top[..., None]), 0.0)
        rescale = jnp.exp(top_score - new_top)
        totals = jnp.sum(weights, axis=-1)
        context_sum = jnp.einsum(
            "kgts,skd->kgtd",
            weights.astype(jnp.bfloat16),
            value_rows,
            preferred_element_type=jnp.float32,
        )
        return (new_top, totals, context_sum)

    skip_piece = (offset + row_count <= earliest) | (offset > latest)
    top_score, totals, context_sum = lax.cond(skip_piece, lambda current: current, update, initial)
    context = (
        (context_sum / totals[..., None])
        .transpose(2, 0, 1, 3)
        .reshape(tok_rows, q_local * HEAD_DIM)
        .astype(jnp.bfloat16)
    )
    vocab_local = w_head.shape[1]
    y_count = lax.psum(1, "y")
    z_count = lax.psum(1, "z")
    z_index = lax.axis_index("z")
    y_index = lax.axis_index("y")
    kv_index = lax.axis_index("kv")
    attn_out = lax.psum(jnp.dot(context, w_o, preferred_element_type=jnp.float32), "kv")
    final_in = rms_norm(stream + RESID_SCALE * attn_out, final_gain).astype(jnp.bfloat16)
    head_rows = lax.all_gather(final_in, "y", axis=0, tiled=True)
    group_rows = head_rows.shape[0]
    head_cols = lax.all_gather(w_head, "z", axis=1, tiled=True)
    mask_cols = lax.all_gather(vocab_mask, "z", axis=0, tiled=True)
    live_mask = mask_cols == 1
    shard_ids = (
        kv_index * (z_count * y_count) + jnp.arange(z_count, dtype=jnp.int32) * y_count + y_index
    )
    columns = (
        shard_ids[:, None] * vocab_local + jnp.arange(vocab_local, dtype=jnp.int32)[None, :]
    ).reshape(-1)
    row_ids = lax.dynamic_slice_in_dim(target_ids, z_index * group_rows, group_rows, 0)
    logits = jnp.dot(head_rows, head_cols, preferred_element_type=jnp.float32) * LOGIT_SCALE
    masked = jnp.where(live_mask[None, :], logits, NEG_FILL)
    top_row = jnp.max(masked, axis=1)
    shifted = jnp.where(live_mask[None, :], masked - top_row[:, None], 0.0)
    expw = jnp.where(live_mask[None, :], jnp.exp(shifted), 0.0)
    target = jnp.sum(jnp.where(row_ids[:, None] == columns[None, :], logits, 0.0), axis=1)
    row_stats = jnp.stack([top_row, jnp.sum(expw, axis=1), jnp.sum(expw * shifted, axis=1), target])
    top_all = lax.pmax(row_stats[0], ("kv", "y"))
    rescale = jnp.exp(row_stats[0] - top_all)
    total_all, spread_all, target_all = lax.psum(
        (
            row_stats[1] * rescale,
            rescale * (row_stats[2] + (row_stats[0] - top_all) * row_stats[1]),
            row_stats[3],
        ),
        ("kv", "y"),
    )
    log_prob = target_all - top_all - jnp.log(total_all)
    entropy = jnp.log(total_all) - spread_all / total_all
    log_probs = lax.dynamic_slice_in_dim(log_prob, y_index * tok_rows, tok_rows, 0)
    entropies = lax.dynamic_slice_in_dim(entropy, y_index * tok_rows, tok_rows, 0)
    return (log_probs, entropies)


def solution(mesh):
    kv_size, seq_size = mesh.devices.shape
    z_size = mesh.shape["seq"] // 4 if mesh.shape["seq"] % 4 == 0 else mesh.shape["seq"]
    y_size = seq_size // z_size
    split_mesh = Mesh(mesh.devices.reshape(kv_size, z_size, y_size), ("kv", "z", "y"))
    seq = ("z", "y")
    in_specs = (
        P(seq, None),
        P(),
        P(None, "kv"),
        P(None, "kv"),
        P(None, "kv"),
        P("kv", None),
        P(),
        P(None, ("kv",) + seq),
        P(),
        P(),
        P(("kv",) + seq),
    )
    out_specs = (P(seq), P(seq))
    return jax.shard_map(
        local, mesh=split_mesh, in_specs=in_specs, out_specs=out_specs, check_vma=False
    )
```

profile of v0, /device:TPU:32, one launch (start us, length us, event | category | flops | bytes accessed | tf_op | source)
XLA Modules:
  0.0 449.0 jit_solution(1061210086343181944)
XLA Ops:
  8.1 0.9 copy.22
  10.0 1.4 fusion.16
  11.3 1.6 convolution_bitcast_fusion
  13.0 1.6 convolution_convert_fusion
  14.9 0.7 copy.23
  19.0 75.5 %all-gather.5.cloned.1.call-done = bf16[6144,128]{1,0:T(8,128)(2,1)} async-done(((bf16[192,128]{1,0:T(8,128)(2,1)}), bf16[6144,128]{1,0:T(8,128)(2,1)}) %all-gather.5.cloned.1.call-update) | async-done | bytes 1572880 | tf_op jit(solution)/shard_map/all_gather | solution.py:87
  94.5 21.4 %conditional.1 = (f32[1,4,192]{2,1,0:T(4,128)S(1)}, f32[1,4,192,64]{2,3,1,0:T(8,128)S(1)}) conditional(s32[]{:T(128)} %bitcast.9, (s32[6144]{0:T(1024)S(1)}, s32[6144]{0:T(1024)S(1)}, s32[192]{0:T(256)S(1)}, s32[192]{0:T(256)S(1)}, bf16[6144,128]{1,0:T(8,128)(2,1)}, /*index=5*/bf16[192,1,4,64]{0,3,2,1:T(8,128)(2,1)S(1)}) %tuple.16, () %tuple.17), branch_computations={%region_3.6_spmd, %region_6.7_spmd} | conditional | flops 1272839424 | bytes 66424336 | solution.py:117
  94.5 1.0 compare_and_fusion
  95.5 2.6 copy.25
  98.1 5.0 %fusion = (f32[4,192]{1,0:T(4,128)S(1)}, f32[6144,192,4]{0,1,2:T(8,128)S(1)}) fusion(pred[192,6144]{1,0:T(8,128)(4,1)S(1)} %compare_and_fusion, bf16[192,1,4,64]{0,3,2,1:T(8,128)(2,1)S(1)} %get-tuple-element.16, bf16[6144,128]{0,1:T(8,128)(2,1)} %copy.25), kind=kOutput, calls=%fused_computation.2 | convolution fusion | flops 618134784 | bytes 20941824 | tf_op jit(solution)/shard_map/cond/branch_0_fun/tkgd,skd->kgts/dot_general | solution.py:97
  103.1 6.3 %fusion.7 = f32[1,4,192,64]{2,3,1,0:T(8,128)S(1)} fusion(f32[6144,192,4]{0,1,2:T(8,128)S(1)} %get-tuple-element.42, f32[4,192]{1,0:T(4,128)S(1)} %broadcast_maximum_fusion, pred[192,6144]{1,0:T(8,128)(4,1)S(1)} %compare_and_fusion, bf16[6144,128]{0,1:T(8,128)(2,1)} %copy.25), kind=kOutput, calls=%fused_computation.9 | convolution fusion | flops 627572736 | bytes 21040128 | tf_op jit(solution)/shard_map/cond/branch_0_fun/kgts,skd->kgtd/dot_general | solution.py:108
  109.4 6.5 %fusion.2 = f32[4,192]{1,0:T(4,128)S(1)} fusion(f32[6144,192,4]{0,1,2:T(8,128)S(1)} %get-tuple-element.42, f32[4,192]{1,0:T(4,128)S(1)} %broadcast_maximum_fusion, pred[192,6144]{1,0:T(8,128)(4,1)S(1)} %compare_and_fusion), kind=kLoop, calls=%fused_computation.4 | loop fusion | flops 23592192 | bytes 20060160 | tf_op jit(solution)/shard_map/cond/branch_0_fun/reduce_sum | solution.py:107
  115.9 1.6 fusion.35
  118.4 67.6 %all-reduce.4.cloned.1.call-done = f32[192,2048]{1,0:T(8,128)} async-done(((f32[192,2048]{1,0:T(8,128)}), f32[192,2048]{1,0:T(8,128)}) %all-reduce.4.cloned.1.call-update) | async-done | bytes 1572880 | tf_op jit(solution)/shard_map/psum | solution.py:130
  186.1 1.7 multiply_reduce_fusion.1
  187.8 2.6 multiply_convert_fusion
  191.9 0.8 dynamic_slice.9
  192.9 14.0 %all-reduce = s32[1544]{0:T(1024)S(1)} all-reduce(s32[1544]{0:T(1024)S(1)} %dynamic-update-slice), channel_id=1, replica_groups=mesh['kv'=8,'z'=8,'y'=4] {'z'}, use_global_device_ids=true, to_apply=%add | all-reduce | flops 1544 | bytes 12352
  207.0 7.8 %reshape.284 = bf16[1544,2048]{1,0:T(8,128)(2,1)} reshape(bf16[8,193,2048]{2,1,0:T(8,128)(2,1)} %all-gather.9.cloned.1.call-done) | data formatting | bytes 12648448
  214.8 22.4 %all-gather.7.cloned.1.call-done = bf16[768,2048]{1,0:T(8,128)(2,1)} async-done(((bf16[192,2048]{1,0:T(8,128)(2,1)}), bf16[768,2048]{1,0:T(8,128)(2,1)}) %all-gather.7.cloned.1.call-update) | async-done | bytes 3145744 | tf_op jit(solution)/shard_map/all_gather | solution.py:132
  237.2 9.8 %select_reduce_fusion.1 = (f32[768]{0:T(1024)S(1)}, f32[768,1544]{0,1:T(8,128)}) fusion(pred[1544]{0:T(1024)(128)(4,1)S(1)} %broadcast_compare_fusion, bf16[768,2048]{1,0:T(8,128)(2,1)} %all-gather.7.cloned.1.call-done, bf16[1544,2048]{1,0:T(8,128)(2,1)} %reshape.284), kind=kOutput, calls=%fused_computation.23 | convolution fusion | flops 4860560384 | bytes 14217736 | tf_op jit(solution)/shard_map/dot_general | solution.py:144
  247.0 64.9 %pmax.7 = f32[768]{0:T(1024)S(1)} all-reduce(f32[768]{0:T(1024)S(1)} %get-tuple-element.53), channel_id=1, replica_groups=mesh['kv'=8,'z'=8,'y'=4] {'kv','y'}, use_global_device_ids=true, to_apply=%region_12.13 | all-reduce | flops 768 | bytes 6144 | tf_op jit(solution)/shard_map/pmax | solution.py:151
  311.9 4.5 %multiply_reduce_fusion = (f32[768]{0:T(1024)S(1)}, f32[768]{0:T(1024)S(1)}, f32[768]{0:T(1024)S(1)}) fusion(f32[768,1544]{0,1:T(8,128)} %get-tuple-element.54, f32[768]{0:T(1024)S(1)} %get-tuple-element.53, pred[1544]{0:T(1024)(128)(4,1)S(1)} %broadcast_compare_fusion, s32[1544]{0:T(1024)S(1)} %add.107, s32[768]{0:T(1024)S(1)} %dynamic_slice.9), kind=kLoop, calls=%fused_computation.18 | loop fusion | flops 13041408 | bytes 4766248 | tf_op jit(solution)/shard_map/reduce_sum | solution.py:150
  316.5 123.8 %all-reduce.1 = (f32[768]{0:T(1024)S(1)}, f32[768]{0:T(1024)S(1)}, f32[768]{0:T(1024)S(1)}) all-reduce(f32[768]{0:T(1024)S(1)} %get-tuple-element.37, f32[768]{0:T(1024)S(1)} %get-tuple-element.48, f32[768]{0:T(1024)S(1)} %get-tuple-element.47), channel_id=1, replica_groups=mesh['kv'=8,'z'=8,'y'=4] {'kv','y'}, use_global_device_ids=true, to_apply=%region_10.11 | all-reduce | flops 2304 | bytes 18432 | tf_op jit(solution)/shard_map/psum | solution.py:153
  (54 shorter events, 6.4 us)
Async XLA Ops:
  8.0 107.9 %copy-start = (bf16[256,2048]{1,0:T(8,128)(2,1)S(1)}, bf16[256,2048]{1,0:T(8,128)(2,1)}, u32[]{:S(2)}) copy-start(bf16[256,2048]{1,0:T(8,128)(2,1)} %param.18) | copy-start | bytes 3145732
  8.0 10.3 %copy-start.1 = (bf16[192,2048]{1,0:T(8,128)(2,1)S(1)}, bf16[192,2048]{1,0:T(8,128)(2,1)}, u32[]{:S(2)}) copy-start(bf16[192,2048]{1,0:T(8,128)(2,1)} %param.13) | copy-start | bytes 2359300
  8.0 10.3 %copy-start.5 = (f32[2048]{0:T(1024)S(1)}, f32[2048]{0:T(1024)}, u32[]{:S(2)}) copy-start(f32[2048]{0:T(1024)} %param.14) | copy-start | bytes 24580
  8.0 10.3 %copy-start.4 = (bf16[2048,256]{1,0:T(8,128)(2,1)S(1)}, bf16[2048,256]{1,0:T(8,128)(2,1)}, u32[]{:S(2)}) copy-start(bf16[2048,256]{1,0:T(8,128)(2,1)} %param.15) | copy-start | bytes 3145732
  8.0 86.5 %all-gather.5.cloned.1.call-start = ((), (), s32[]{:S(2)}) async-start(), calls=%async_computation | async-start | bytes 1622016 | tf_op jit(solution)/shard_map/all_gather | solution.py:87
  15.6 170.5 %all-reduce.4.cloned.1.call-start = ((), (), s32[]{:S(2)}) async-start(), calls=%async_computation.1 | async-start | bytes 3145728 | tf_op jit(solution)/shard_map/psum | solution.py:130
  115.9 72.0 %copy-start.2 = (f32[2048]{0:T(1024)S(1)}, f32[2048]{0:T(1024)}, u32[]{:S(2)}) copy-start(f32[2048]{0:T(1024)} %param.19) | copy-start | bytes 24580
  117.6 73.1 %copy-start.6 = (u32[256]{0:T(256)S(1)}, u32[256]{0:T(256)}, u32[]{:S(2)}) copy-start(u32[256]{0:T(256)} %constant.73) | copy-start | bytes 3076
  117.6 75.1 %copy-start.3 = (s32[193]{0:T(256)S(1)}, s32[193]{0:T(256)}, u32[]{:S(2)}) copy-start(s32[193]{0:T(256)} %param.23) | copy-start | bytes 2320
  117.6 89.4 %all-gather.9.cloned.1.call-start = ((), (), s32[]{:S(2)}) async-start(), calls=%async_computation.3 | async-start | bytes 7372800 | tf_op jit(solution)/shard_map/all_gather | solution.py:134
  118.2 119.0 %all-gather.7.cloned.1.call-start = ((), (), s32[]{:S(2)}) async-start(), calls=%async_computation.2 | async-start | bytes 3932160 | tf_op jit(solution)/shard_map/all_gather | solution.py:132
Sparse Core Ops, SparseCore 0:
  15.7 78.7 all-gather.4
  117.7 68.2 all-reduce.3
Sparse Core Ops, SparseCore 1:
  119.9 73.3 all-gather.8
  194.9 42.3 all-gather.6
where the time goes:
time: 450 us; the launch traced here: 449 us
  blocking collectives  203 us (45%)
  waiting for transfers between devices  166 us (37%)
  matrix products  26.6 us (6%)
  other arithmetic  19.3 us (4%)
  between operations  17.7 us (4%)
  local copies, waits for them, and re-layouts  16.2 us (4%)
    psum x1, blocking collectives, local(): lax.psum((row_stats[1] * rescale, rescale * (row_stats[2] + (row_stats[0]...  124 us
    all_gather x1, waiting for transfers between devices, local(): shard_rows = lax.all_gather(packed, ('z', 'y'), axis=0, tiled=True)  75.5 us
    psum x1, waiting for transfers between devices, local(): lax.psum(jnp.dot(context, w_o, preferred_element_type=jnp.float32), 'kv')  67.6 us
    pmax x1, blocking collectives, local(): top_all = lax.pmax(row_stats[0], ('kv', 'y'))  64.9 us
    all_gather x1, waiting for transfers between devices, local(): head_rows = lax.all_gather(final_in, 'y', axis=0, tiled=True)  22.4 us
    unnamed x1, blocking collectives  14 us
    dot_general x1, matrix products, local(): jnp.dot(head_rows, head_cols, preferred_element_type=jnp.float32)  9.77 us
  transfers between devices with their start and end apart: 4, of which 3 were waited for; matrix products, arithmetic and copies ran while one was open for 4% of the time, Pallas kernels for 0%

commit v1 on v0

--- a/solution.py
+++ b/solution.py
@@ -3,6 +3,7 @@
 import jax.numpy as jnp
 from jax import lax
 from jax.sharding import Mesh, PartitionSpec as P
+from jax.lax import all_gather
 
 HEAD_DIM = 64
 ROPE_THETA = 10000000.0
@@ -127,7 +128,8 @@
     z_index = lax.axis_index("z")
     y_index = lax.axis_index("y")
     kv_index = lax.axis_index("kv")
-    attn_out = lax.psum(jnp.dot(context, w_o, preferred_element_type=jnp.float32), "kv")
+    patch = jnp.dot(context, w_o, preferred_element_type=jnp.float32)
+    attn_out = jnp.sum(all_gather(patch, "kv"), 0)
     final_in = rms_norm(stream + RESID_SCALE * attn_out, final_gain).astype(jnp.bfloat16)
     head_rows = lax.all_gather(final_in, "y", axis=0, tiled=True)
     group_rows = head_rows.shape[0]

time: 450 us -> 518 us (1.15)
  waiting for transfers between devices: 166 us -> 234 us
    psum x1 -> x0, waiting for transfers between devices: 67.6 us -> none  [local(): lax.psum(jnp.dot(context, w_o, preferred_element_type=jnp.float32), 'kv')]
    all_gather x0 -> x1, waiting for transfers between devices: none -> 67.2 us  [local(): attn_out = jnp.sum(all_gather(patch, 'kv'), 0)]
    all_gather x1, waiting for transfers between devices: 0.03 us -> 54.2 us  [local(): head_cols = lax.all_gather(w_head, 'z', axis=1, tiled=True)]
    all_gather x1, waiting for transfers between devices: 22.4 us -> 36.5 us  [local(): head_rows = lax.all_gather(final_in, 'y', axis=0, tiled=True)]
    reduce_sum x0 -> x1, other arithmetic: none -> 6.03 us  [local(): attn_out = jnp.sum(all_gather(patch, 'kv'), 0)]
  transfers between devices with their start and end apart: 4 -> 4, of which waited for: 3 -> 4; matrix products, arithmetic and copies ran while one was open for 4% -> 4% of each run, Pallas kernels for 0% -> 0%
where the time goes in v1:
time: 518 us
  waiting for transfers between devices  234 us (45%)
  blocking collectives  203 us (39%)
  matrix products  26.6 us (5%)
  other arithmetic  22.5 us (4%)
  between operations  16 us (3%)
  local copies, waits for them, and re-layouts  15.7 us (3%)
    psum x1, blocking collectives, local(): lax.psum((row_stats[1] * rescale, rescale * (row_stats[2] + (row_stats[0]...  124 us
    all_gather x1, waiting for transfers between devices, local(): shard_rows = lax.all_gather(packed, ('z', 'y'), axis=0, tiled=True)  75.5 us
    all_gather x1, waiting for transfers between devices, local(): attn_out = jnp.sum(all_gather(patch, 'kv'), 0)  67.2 us
    pmax x1, blocking collectives, local(): top_all = lax.pmax(row_stats[0], ('kv', 'y'))  65 us
    all_gather x1, waiting for transfers between devices, local(): head_cols = lax.all_gather(w_head, 'z', axis=1, tiled=True)  54.2 us
    all_gather x1, waiting for transfers between devices, local(): head_rows = lax.all_gather(final_in, 'y', axis=0, tiled=True)  36.5 us
    unnamed x1, blocking collectives  13.8 us
  transfers between devices with their start and end apart: 4, of which 4 were waited for; matrix products, arithmetic and copies ran while one was open for 4% of the time, Pallas kernels for 0%

profile of v1, /device:TPU:32, one launch (start us, length us, event | category | flops | bytes accessed | tf_op | source)
XLA Modules:
  0.0 517.7 jit_solution(13739986480736484651)
XLA Ops:
  7.3 0.9 copy.22
  9.1 1.4 fusion.16
  10.5 1.6 convolution_bitcast_fusion
  12.2 1.6 convolution_convert_fusion
  18.2 75.5 %all-gather.7.cloned.1.call-done = bf16[6144,128]{1,0:T(8,128)(2,1)} async-done(((bf16[192,128]{1,0:T(8,128)(2,1)}), bf16[6144,128]{1,0:T(8,128)(2,1)}) %all-gather.7.cloned.1.call-update) | async-done | bytes 1572880 | tf_op jit(solution)/shard_map/all_gather | solution.py:88
  93.7 21.4 %conditional.1 = (f32[1,4,192]{2,1,0:T(4,128)S(1)}, f32[1,4,192,64]{2,3,1,0:T(8,128)S(1)}) conditional(s32[]{:T(128)} %bitcast.9, (s32[6144]{0:T(1024)S(1)}, s32[6144]{0:T(1024)S(1)}, s32[192]{0:T(256)S(1)}, s32[192]{0:T(256)S(1)}, bf16[6144,128]{1,0:T(8,128)(2,1)}, /*index=5*/bf16[192,1,4,64]{0,3,2,1:T(8,128)(2,1)S(1)}) %tuple.16, () %tuple.17), branch_computations={%region_3.6_spmd, %region_6.7_spmd} | conditional | flops 1272839424 | bytes 66424336 | solution.py:118
  93.7 1.0 compare_and_fusion
  94.7 2.6 copy.25
  97.3 5.0 fusion
  102.3 6.3 %fusion.7 = f32[1,4,192,64]{2,3,1,0:T(8,128)S(1)} fusion(f32[6144,192,4]{0,1,2:T(8,128)S(1)} %get-tuple-element.42, f32[4,192]{1,0:T(4,128)S(1)} %broadcast_maximum_fusion, pred[192,6144]{1,0:T(8,128)(4,1)S(1)} %compare_and_fusion, bf16[6144,128]{0,1:T(8,128)(2,1)} %copy.25), kind=kOutput, calls=%fused_computation.9 | convolution fusion | flops 627572736 | bytes 21040128 | tf_op jit(solution)/shard_map/cond/branch_0_fun/kgts,skd->kgtd/dot_general | solution.py:109
  108.6 6.5 %fusion.2 = f32[4,192]{1,0:T(4,128)S(1)} fusion(f32[6144,192,4]{0,1,2:T(8,128)S(1)} %get-tuple-element.42, f32[4,192]{1,0:T(4,128)S(1)} %broadcast_maximum_fusion, pred[192,6144]{1,0:T(8,128)(4,1)S(1)} %compare_and_fusion), kind=kLoop, calls=%fused_computation.4 | loop fusion | flops 23592192 | bytes 20060160 | tf_op jit(solution)/shard_map/cond/branch_0_fun/reduce_sum | solution.py:108
  115.1 1.6 fusion.35
  117.7 67.2 %all-gather.11.cloned.1.call-done = f32[1536,2048]{1,0:T(8,128)} async-done(((f32[192,2048]{1,0:T(8,128)}), f32[1536,2048]{1,0:T(8,128)}) %all-gather.11.cloned.1.call-update) | async-done | bytes 12582928 | tf_op jit(solution)/shard_map/all_gather | solution.py:132
  184.9 6.0 %reduce_sum.66 = f32[192,2048]{1,0:T(8,128)S(1)} reduce(f32[8,192,2048]{2,1,0:T(8,128)} %bitcast.67, f32[]{:T(128)} %constant.60.clone.1), dimensions={0}, to_apply=%region_7.8 | reduce | flops 2752512 | bytes 14155780 | tf_op jit(solution)/shard_map/reduce_sum | solution.py:132
  191.3 1.2 multiply_convert_fusion
  194.0 0.8 dynamic_slice.9
  195.0 13.8 %all-reduce = s32[1544]{0:T(1024)S(1)} all-reduce(s32[1544]{0:T(1024)S(1)} %dynamic-update-slice), channel_id=1, replica_groups=mesh['kv'=8,'z'=8,'y'=4] {'z'}, use_global_device_ids=true, to_apply=%add | all-reduce | flops 1544 | bytes 12352
  208.8 54.2 %all-gather.13.cloned.1.call-done = bf16[8,193,2048]{2,1,0:T(8,128)(2,1)} async-done(((bf16[1,193,2048]{2,1,0:T(8,128)(2,1)}), bf16[8,193,2048]{2,1,0:T(8,128)(2,1)}) %all-gather.13.cloned.1.call-update) | async-done | bytes 6324240 | tf_op jit(solution)/shard_map/all_gather | solution.py:136
  262.9 7.4 %reshape.285 = bf16[1544,2048]{1,0:T(8,128)(2,1)} reshape(bf16[8,193,2048]{2,1,0:T(8,128)(2,1)} %all-gather.13.cloned.1.call-done) | data formatting | bytes 12648448
  270.3 36.5 %all-gather.9.cloned.1.call-done = bf16[768,2048]{1,0:T(8,128)(2,1)} async-done(((bf16[192,2048]{1,0:T(8,128)(2,1)}), bf16[768,2048]{1,0:T(8,128)(2,1)}) %all-gather.9.cloned.1.call-update) | async-done | bytes 3145744 | tf_op jit(solution)/shard_map/all_gather | solution.py:134
  306.8 9.8 %select_reduce_fusion.1 = (f32[768]{0:T(1024)S(1)}, f32[768,1544]{0,1:T(8,128)}) fusion(pred[1544]{0:T(1024)(128)(4,1)S(1)} %broadcast_compare_fusion, bf16[768,2048]{1,0:T(8,128)(2,1)} %all-gather.9.cloned.1.call-done, bf16[1544,2048]{1,0:T(8,128)(2,1)} %reshape.285), kind=kOutput, calls=%fused_computation.23 | convolution fusion | flops 4860560384 | bytes 14217736 | tf_op jit(solution)/shard_map/dot_general | solution.py:146
  316.6 65.0 %pmax.7 = f32[768]{0:T(1024)S(1)} all-reduce(f32[768]{0:T(1024)S(1)} %get-tuple-element.53), channel_id=1, replica_groups=mesh['kv'=8,'z'=8,'y'=4] {'kv','y'}, use_global_device_ids=true, to_apply=%region_12.13 | all-reduce | flops 768 | bytes 6144 | tf_op jit(solution)/shard_map/pmax | solution.py:153
  381.6 4.5 multiply_reduce_fusion
  386.1 123.8 %all-reduce.1 = (f32[768]{0:T(1024)S(1)}, f32[768]{0:T(1024)S(1)}, f32[768]{0:T(1024)S(1)}) all-reduce(f32[768]{0:T(1024)S(1)} %get-tuple-element.37, f32[768]{0:T(1024)S(1)} %get-tuple-element.48, f32[768]{0:T(1024)S(1)} %get-tuple-element.47), channel_id=1, replica_groups=mesh['kv'=8,'z'=8,'y'=4] {'kv','y'}, use_global_device_ids=true, to_apply=%region_10.11 | all-reduce | flops 2304 | bytes 18432 | tf_op jit(solution)/shard_map/psum | solution.py:155
  (55 shorter events, 7.6 us)
Async XLA Ops:
  7.2 107.9 %copy-start = (bf16[256,2048]{1,0:T(8,128)(2,1)S(1)}, bf16[256,2048]{1,0:T(8,128)(2,1)}, u32[]{:S(2)}) copy-start(bf16[256,2048]{1,0:T(8,128)(2,1)} %param.18) | copy-start | bytes 3145732
  7.2 10.3 %copy-start.1 = (bf16[192,2048]{1,0:T(8,128)(2,1)S(1)}, bf16[192,2048]{1,0:T(8,128)(2,1)}, u32[]{:S(2)}) copy-start(bf16[192,2048]{1,0:T(8,128)(2,1)} %param.13) | copy-start | bytes 2359300
  7.2 10.3 %copy-start.5 = (f32[2048]{0:T(1024)S(1)}, f32[2048]{0:T(1024)}, u32[]{:S(2)}) copy-start(f32[2048]{0:T(1024)} %param.14) | copy-start | bytes 24580
  7.2 10.3 %copy-start.4 = (bf16[2048,256]{1,0:T(8,128)(2,1)S(1)}, bf16[2048,256]{1,0:T(8,128)(2,1)}, u32[]{:S(2)}) copy-start(bf16[2048,256]{1,0:T(8,128)(2,1)} %param.15) | copy-start | bytes 3145732
  7.2 86.5 %all-gather.7.cloned.1.call-start = ((), (), s32[]{:S(2)}) async-start(), calls=%async_computation | async-start | bytes 1622016 | tf_op jit(solution)/shard_map/all_gather | solution.py:88
  14.8 170.1 %all-gather.11.cloned.1.call-start = ((), (), s32[]{:S(2)}) async-start(), calls=%async_computation.2 | async-start | bytes 14155776 | tf_op jit(solution)/shard_map/all_gather | solution.py:132
  116.7 146.2 %all-gather.13.cloned.1.call-start = ((), (), s32[]{:S(2)}) async-start(), calls=%async_computation.3 | async-start | bytes 7372800 | tf_op jit(solution)/shard_map/all_gather | solution.py:136
  117.4 189.4 %all-gather.9.cloned.1.call-start = ((), (), s32[]{:S(2)}) async-start(), calls=%async_computation.1 | async-start | bytes 3932160 | tf_op jit(solution)/shard_map/all_gather | solution.py:134
  184.9 6.4 %copy-start.2 = (f32[2048]{0:T(1024)S(1)}, f32[2048]{0:T(1024)}, u32[]{:S(2)}) copy-start(f32[2048]{0:T(1024)} %param.19) | copy-start | bytes 24580
  190.9 1.8 copy-start.6
  190.9 3.8 copy-start.3
Sparse Core Ops, SparseCore 0:
  14.9 78.7 all-gather.6
  116.8 67.9 all-gather.10
  186.7 76.1 all-gather.12
  264.6 42.1 all-gather.8
